TPU v7x, 512 devices: a whole 4x8x8 slice. The times are simulated.
512 devices in a mesh: tm: 64 (over y, x, core), head: 8 (over z).
Axes of the slice: x: 4, y: 8, z: 8, core: 2. Of those that a mesh axis runs over, the one named last changes fastest.
Arguments:
- queries: bfloat16 [24576, 5120], P('tm', 'head')
- keys: bfloat16 [24576, 5120], P('tm', 'head')
- values: bfloat16 [24576, 5120], P('tm', 'head')
- text_keys: bfloat16 [512, 5120], P('tm', 'head'), may hold values from -6 to 6
- text_values: bfloat16 [512, 5120], P('tm', 'head')
- out_weight: bfloat16 [5120, 5120], P('head', 'tm'), may hold values from -0.25 to 0.25
- windows: int32 [64], replicated, may hold values from 0 to 4, as said below
- lengths: int32 [64], replicated, may hold values from 96 to 384, as said below
Outputs:
- mixed: bfloat16 [24576, 5120], P('tm', 'head')
Inputs may be any that keep to these rules, and one draw needn't show every extreme that they name: windows reach 4 for some frame in every draw. `lengths`: some frame is full in every draw.
All inputs are finite; a program needn't handle non-finite values.
Results may differ from a plain program's by a relative error of at most 0.014.
Values may be sent and summed in bfloat16 or wider, within the bound.
No kernel may reach another device: no remote copies, remote signals or barrier semaphores. Data moves between devices by JAX's collectives and lax.ppermute only.
A program may use at most 64 MiB of HBM per device.

v0:
```python
import math
import jax
import jax.numpy as jnp
from jax import lax
from jax.sharding import PartitionSpec as P

HD = 128
WIN = 4


def from_behind(value, axis, steps):
    count = lax.axis_size(axis)
    initial, last = (max(0, -steps), min(count, count - steps))
    return lax.ppermute(value, axis, [(source, source + steps) for source in range(initial, last)])


def on_device(queries, keys, values, text_keys, text_values, out_weight, windows, lengths):
    rows = queries.shape[0]
    width = queries.shape[1]
    local_heads = width // HD
    scale = 1.0 / math.sqrt(HD)
    position = lax.axis_index("tm")
    text_k, text_v = (
        lax.all_gather(text_keys, "tm", axis=0, tiled=True),
        lax.all_gather(text_values, "tm", axis=0, tiled=True),
    )
    key_list = [keys]
    value_list = [values]
    for step in range(1, WIN + 1):
        moved_k, moved_v = from_behind((keys, values), "tm", step)
        key_list.append(moved_k)
        value_list.append(moved_v)
    token_ids = jnp.arange(rows, dtype=jnp.int32)
    own_window = windows[position]
    mask_list = []
    for step in range(WIN + 1):
        source = position - step
        usable = (step <= own_window) & (source >= 0)
        source_len = lengths[jnp.maximum(source, 0)]
        mask_list.append(usable & (token_ids < source_len))
    mask_list.append(jnp.ones((text_k.shape[0],), bool))
    key_mask = jnp.concatenate(mask_list)
    all_keys = jnp.concatenate(key_list + [text_k], axis=0)
    all_values = jnp.concatenate(value_list + [text_v], axis=0)
    head_outputs = []
    for head_index in range(local_heads):
        lower = head_index * HD
        query_h = queries[:, lower : lower + HD]
        key_h = all_keys[:, lower : lower + HD]
        value_h = all_values[:, lower : lower + HD]
        scores = (
            lax.dot_general(
                query_h, key_h, (((1,), (1,)), ((), ())), preferred_element_type=jnp.float32
            )
            * scale
        )
        scores = jnp.where(key_mask[None, :], scores, -jnp.inf)
        top = jnp.max(scores, axis=-1, keepdims=True)
        weights = jnp.exp(scores - top)
        total = jnp.sum(weights, axis=-1, keepdims=True)
        attended = (
            jnp.dot(weights.astype(jnp.bfloat16), value_h, preferred_element_type=jnp.float32)
            / total
        )
        head_outputs.append(attended.astype(jnp.bfloat16))
    attended_all = jnp.concatenate(head_outputs, axis=1)
    partial_out = jnp.dot(
        attended_all,
        lax.all_gather(out_weight, "tm", axis=1, tiled=True),
        preferred_element_type=jnp.float32,
    )
    return lax.psum_scatter(
        partial_out.astype(jnp.bfloat16), "head", scatter_dimension=1, tiled=True
    )


def solution(mesh):
    return jax.shard_map(
        on_device,
        mesh=mesh,
        in_specs=(
            P("tm", "head"),
            P("tm", "head"),
            P("tm", "head"),
            P("tm", "head"),
            P("tm", "head"),
            P("head", "tm"),
            P(),
            P(),
        ),
        out_specs=P("tm", "head"),
        check_vma=False,
    )
```

profile of v0, /device:TPU:1, one launch (start us, length us, event | category | flops | bytes accessed | tf_op | source)
XLA Modules:
  0.0 300.5 jit_solution(977108429921644657)
XLA Ops:
  6.5 0.7 all-gather.2.cloned.1.call-update
  7.3 4.5 %collective-permute-start = (bf16[384,640]{1,0:T(8,128)(2,1)}, bf16[384,640]{1,0:T(8,128)(2,1)S(1)}, u32[]{:S(2)}, u32[]{:S(2)}) collective-permute-start(bf16[384,640]{1,0:T(8,128)(2,1)} %param.9), channel_id=1, source_target_pairs={{0,8},{8,16},{16,24},{24,32},{32,40},{40,48},{48,56},{56,64},{64,7... | collective-permute-start | bytes 1474568 | tf_op jit(solution)/shard_map/ppermute | solution.py:14
  11.8 3.1 %collective-permute-start.1 = (bf16[384,640]{1,0:T(8,128)(2,1)}, bf16[384,640]{1,0:T(8,128)(2,1)S(1)}, u32[]{:S(2)}, u32[]{:S(2)}) collective-permute-start(bf16[384,640]{1,0:T(8,128)(2,1)} %param.9), channel_id=1, source_target_pairs={{0,16},{8,24},{16,32},{24,40},{32,48},{40,56},{48,64},{56,72},{64,... | collective-permute-start | bytes 1474568 | tf_op jit(solution)/shard_map/ppermute | solution.py:14
  15.0 3.4 %collective-permute-start.2 = (bf16[384,640]{1,0:T(8,128)(2,1)}, bf16[384,640]{1,0:T(8,128)(2,1)S(1)}, u32[]{:S(2)}, u32[]{:S(2)}) collective-permute-start(bf16[384,640]{1,0:T(8,128)(2,1)} %param.9), channel_id=1, source_target_pairs={{0,24},{8,32},{16,40},{24,48},{32,56},{40,64},{48,72},{56,80},{64,... | collective-permute-start | bytes 1474568 | tf_op jit(solution)/shard_map/ppermute | solution.py:14
  18.4 3.4 %collective-permute-start.3 = (bf16[384,640]{1,0:T(8,128)(2,1)}, bf16[384,640]{1,0:T(8,128)(2,1)S(1)}, u32[]{:S(2)}, u32[]{:S(2)}) collective-permute-start(bf16[384,640]{1,0:T(8,128)(2,1)} %param.9), channel_id=1, source_target_pairs={{0,32},{8,40},{16,48},{24,56},{32,64},{40,72},{48,80},{56,88},{64,... | collective-permute-start | bytes 1474568 | tf_op jit(solution)/shard_map/ppermute | solution.py:14
  21.9 3.7 %collective-permute-start.4 = (bf16[384,640]{1,0:T(8,128)(2,1)}, bf16[384,640]{1,0:T(8,128)(2,1)S(1)}, u32[]{:S(2)}, u32[]{:S(2)}) collective-permute-start(bf16[384,640]{1,0:T(8,128)(2,1)} %param.10), channel_id=1, source_target_pairs={{0,8},{8,16},{16,24},{24,32},{32,40},{40,48},{48,56},{56,64},{64,7... | collective-permute-start | bytes 1474568 | tf_op jit(solution)/shard_map/ppermute | solution.py:14
  25.6 1.2 dynamic_slice.18
  30.1 1.5 fusion.95
  31.6 0.6 fusion.90
  32.2 0.3 dynamic-update-slice.17
  32.4 0.6 fusion.91
  33.1 0.3 dynamic-update-slice.18
  33.3 0.6 fusion.92
  34.0 0.3 dynamic-update-slice.19
  34.2 0.6 fusion.93
  34.9 0.3 dynamic-update-slice.20
  35.1 0.7 fusion.94
  35.8 0.3 dynamic-update-slice.21
  36.0 0.2 dynamic-update-slice.22
  36.3 74.3 %all_gather.9 = bf16[512,640]{1,0:T(8,128)(2,1)S(1)} all-gather(bf16[8,640]{1,0:T(8,128)(2,1)} %param.11), channel_id=1, replica_groups=mesh['tm'=64,'head'=8] {'tm'}, dimensions={0}, use_global_device_ids=true | all-gather | bytes 665600 | tf_op jit(solution)/shard_map/all_gather | solution.py:24
  110.6 48.6 %all_gather.10 = bf16[512,640]{1,0:T(8,128)(2,1)S(1)} all-gather(bf16[8,640]{1,0:T(8,128)(2,1)} %param.12), channel_id=1, replica_groups=mesh['tm'=64,'head'=8] {'tm'}, dimensions={0}, use_global_device_ids=true | all-gather | bytes 665600 | tf_op jit(solution)/shard_map/all_gather | solution.py:25
  159.3 1.1 constant_dynamic-update-slice_fusion.5
  160.3 1.1 constant_dynamic-update-slice_fusion.11
  161.4 2.3 collective-permute-start.5
  163.8 4.6 %collective-permute-start.6 = (bf16[384,640]{1,0:T(8,128)(2,1)S(1)}, bf16[384,640]{1,0:T(8,128)(2,1)S(1)}, u32[]{:S(2)}, u32[]{:S(2)}) collective-permute-start(bf16[384,640]{1,0:T(8,128)(2,1)S(1)} %copy-done), channel_id=1, source_target_pairs={{0,24},{8,32},{16,40},{24,48},{32,56},{40,64},{48,72},{56,80},{64,... | collective-permute-start | bytes 1474568 | tf_op jit(solution)/shard_map/ppermute | solution.py:14
  168.6 2.3 collective-permute-start.7
  171.1 3.4 %collective-permute-done.5 = bf16[384,640]{1,0:T(8,128)(2,1)S(1)} collective-permute-done((bf16[384,640]{1,0:T(8,128)(2,1)}, bf16[384,640]{1,0:T(8,128)(2,1)S(1)}, u32[]{:S(2)}, u32[]{:S(2)}) %collective-permute-start.5) | collective-permute-done | bytes 491552 | tf_op jit(solution)/shard_map/ppermute | solution.py:14
  174.5 10.4 %collective-permute-done.6 = bf16[384,640]{1,0:T(8,128)(2,1)S(1)} collective-permute-done((bf16[384,640]{1,0:T(8,128)(2,1)S(1)}, bf16[384,640]{1,0:T(8,128)(2,1)S(1)}, u32[]{:S(2)}, u32[]{:S(2)}) %collective-permute-start.6) | collective-permute-done | bytes 491552 | tf_op jit(solution)/shard_map/ppermute | solution.py:14
  185.0 10.5 %collective-permute-done.7 = bf16[384,640]{1,0:T(8,128)(2,1)S(1)} collective-permute-done((bf16[384,640]{1,0:T(8,128)(2,1)S(1)}, bf16[384,640]{1,0:T(8,128)(2,1)S(1)}, u32[]{:S(2)}, u32[]{:S(2)}) %collective-permute-start.7) | collective-permute-done | bytes 491552 | tf_op jit(solution)/shard_map/ppermute | solution.py:14
  195.7 0.9 fusion.96
  196.6 0.6 fusion.5
  197.3 0.9 fusion.97
  198.1 0.6 fusion.7
  198.8 0.9 fusion.98
  199.7 0.6 fusion.9
  200.3 0.9 fusion.99
  201.2 0.6 fusion.11
  201.8 0.9 fusion.100
  202.7 0.6 fusion.13
  203.4 0.7 fusion.72
  204.1 0.7 fusion.66
  204.8 0.8 fusion.60
  205.6 0.7 fusion.54
  206.4 0.7 fusion.48
  207.1 8.9 %convolution_convert_fusion = bf16[384,5120]{1,0:T(8,128)(2,1)} fusion(bf16[384,640]{1,0:T(8,128)(2,1)S(1)} %fusion.48, bf16[640,5120]{0,1:T(8,128)(2,1)} %all-gather.2.cloned.1.call-done), kind=kOutput, calls=%fused_computation | convolution fusion | flops 2518548480 | bytes 10977280 | tf_op jit(solution)/shard_map/dot_general | solution.py:67
  216.1 6.3 %copy.9 = bf16[384,5120]{0,1:T(8,128)(2,1)} copy(bf16[384,5120]{1,0:T(8,128)(2,1)} %convolution_convert_fusion) | data formatting | bytes 7864320
  222.4 69.3 %reduce-scatter.4.cloned.1.call-done = bf16[640,384]{1,0:T(8,128)(2,1)} async-done(((bf16[5120,384]{1,0:T(8,128)(2,1)}), bf16[640,384]{1,0:T(8,128)(2,1)}) %reduce-scatter.4.cloned.1.call-update) | async-done | bytes 491536
  291.6 2.0 copy.10
  (25 shorter events, 0.8 us)
Async XLA Ops:
  6.5 157.3 %copy-start = (bf16[384,640]{1,0:T(8,128)(2,1)S(1)}, bf16[384,640]{1,0:T(8,128)(2,1)}, u32[]{:S(2)}) copy-start(bf16[384,640]{1,0:T(8,128)(2,1)} %param.10) | copy-start | bytes 1474564
  6.5 200.6 %all-gather.2.cloned.1.call-start = ((), (), s32[]{:S(2)}) async-start(), calls=%async_computation.1 | async-start | bytes 6656000 | tf_op jit(solution)/shard_map/all_gather | solution.py:69
  7.3 284.4 %reduce-scatter.4.cloned.1.call-start = ((), (), s32[]{:S(2)}) async-start(), calls=%async_computation.2 | async-start | bytes 4423680
  7.3 154.1 %collective-permute-start = (bf16[384,640]{1,0:T(8,128)(2,1)}, bf16[384,640]{1,0:T(8,128)(2,1)S(1)}, u32[]{:S(2)}, u32[]{:S(2)}) collective-permute-start(bf16[384,640]{1,0:T(8,128)(2,1)} %param.9), channel_id=1, source_target_pairs={{0,8},{8,16},{16,24},{24,32},{32,40},{40,48},{48,56},{56,64},{64,7... | collective-permute-start | bytes 1474568 | tf_op jit(solution)/shard_map/ppermute | solution.py:14
  11.8 152.0 %collective-permute-start.1 = (bf16[384,640]{1,0:T(8,128)(2,1)}, bf16[384,640]{1,0:T(8,128)(2,1)S(1)}, u32[]{:S(2)}, u32[]{:S(2)}) collective-permute-start(bf16[384,640]{1,0:T(8,128)(2,1)} %param.9), channel_id=1, source_target_pairs={{0,16},{8,24},{16,32},{24,40},{32,48},{40,56},{48,64},{56,72},{64,... | collective-permute-start | bytes 1474568 | tf_op jit(solution)/shard_map/ppermute | solution.py:14
  15.0 153.6 %collective-permute-start.2 = (bf16[384,640]{1,0:T(8,128)(2,1)}, bf16[384,640]{1,0:T(8,128)(2,1)S(1)}, u32[]{:S(2)}, u32[]{:S(2)}) collective-permute-start(bf16[384,640]{1,0:T(8,128)(2,1)} %param.9), channel_id=1, source_target_pairs={{0,24},{8,32},{16,40},{24,48},{32,56},{40,64},{48,72},{56,80},{64,... | collective-permute-start | bytes 1474568 | tf_op jit(solution)/shard_map/ppermute | solution.py:14
  18.4 152.5 %collective-permute-start.3 = (bf16[384,640]{1,0:T(8,128)(2,1)}, bf16[384,640]{1,0:T(8,128)(2,1)S(1)}, u32[]{:S(2)}, u32[]{:S(2)}) collective-permute-start(bf16[384,640]{1,0:T(8,128)(2,1)} %param.9), channel_id=1, source_target_pairs={{0,32},{8,40},{16,48},{24,56},{32,64},{40,72},{48,80},{56,88},{64,... | collective-permute-start | bytes 1474568 | tf_op jit(solution)/shard_map/ppermute | solution.py:14
  21.9 149.1 %collective-permute-start.4 = (bf16[384,640]{1,0:T(8,128)(2,1)}, bf16[384,640]{1,0:T(8,128)(2,1)S(1)}, u32[]{:S(2)}, u32[]{:S(2)}) collective-permute-start(bf16[384,640]{1,0:T(8,128)(2,1)} %param.10), channel_id=1, source_target_pairs={{0,8},{8,16},{16,24},{24,32},{32,40},{40,48},{48,56},{56,64},{64,7... | collective-permute-start | bytes 1474568 | tf_op jit(solution)/shard_map/ppermute | solution.py:14
  161.4 13.1 %collective-permute-start.5 = (bf16[384,640]{1,0:T(8,128)(2,1)}, bf16[384,640]{1,0:T(8,128)(2,1)S(1)}, u32[]{:S(2)}, u32[]{:S(2)}) collective-permute-start(bf16[384,640]{1,0:T(8,128)(2,1)} %param.10), channel_id=1, source_target_pairs={{0,16},{8,24},{16,32},{24,40},{32,48},{40,56},{48,64},{56,72},{64,... | collective-permute-start | bytes 1474568 | tf_op jit(solution)/shard_map/ppermute | solution.py:14
  163.8 21.1 %collective-permute-start.6 = (bf16[384,640]{1,0:T(8,128)(2,1)S(1)}, bf16[384,640]{1,0:T(8,128)(2,1)S(1)}, u32[]{:S(2)}, u32[]{:S(2)}) collective-permute-start(bf16[384,640]{1,0:T(8,128)(2,1)S(1)} %copy-done), channel_id=1, source_target_pairs={{0,24},{8,32},{16,40},{24,48},{32,56},{40,64},{48,72},{56,80},{64,... | collective-permute-start | bytes 1474568 | tf_op jit(solution)/shard_map/ppermute | solution.py:14
  168.6 26.9 %collective-permute-start.7 = (bf16[384,640]{1,0:T(8,128)(2,1)S(1)}, bf16[384,640]{1,0:T(8,128)(2,1)S(1)}, u32[]{:S(2)}, u32[]{:S(2)}) collective-permute-start(bf16[384,640]{1,0:T(8,128)(2,1)S(1)} %copy-done), channel_id=1, source_target_pairs={{0,32},{8,40},{16,48},{24,56},{32,64},{40,72},{48,80},{56,88},{64,... | collective-permute-start | bytes 1474568 | tf_op jit(solution)/shard_map/ppermute | solution.py:14
  170.9 24.8 %copy-start.1 = (bf16[384,640]{1,0:T(8,128)(2,1)S(1)}, bf16[384,640]{1,0:T(8,128)(2,1)}, u32[]{:S(2)}) copy-start(bf16[384,640]{1,0:T(8,128)(2,1)} %param.8) | copy-start | bytes 1474564
Sparse Core Ops, SparseCore 0:
  10.6 113.0 all-gather.1
  222.5 69.0 reduce-scatter.3
where the time goes:
time: 301 us; the launch traced here: 300 us
  blocking collectives  123 us (41%)
  waiting for transfers between devices  94.2 us (31%)
  starting transfers between devices  27.5 us (9%)
  matrix products  17.1 us (6%)
  between operations  17 us (6%)
  local copies, waits for them, and re-layouts  15.4 us (5%)
  other arithmetic  6.31 us (2%)
    all_gather x1, blocking collectives, on_device(): lax.all_gather(text_keys, 'tm', axis=0, tiled=True)  74.3 us
    unnamed x3, waiting for transfers between devices  70 us
    all_gather x1, blocking collectives, on_device(): lax.all_gather(text_values, 'tm', axis=0, tiled=True)  48.6 us
    ppermute x8, starting transfers between devices, from_behind(): lax.ppermute(value, axis, [(source, source + steps) for source in range(i...  27.5 us
    ppermute x8, waiting for transfers between devices, from_behind(): lax.ppermute(value, axis, [(source, source + steps) for source in range(i...  24.2 us
    unnamed x21, local copies, waits for them, and re-layouts  12.2 us
    dot_general x1, matrix products, on_device(): jnp.dot(attended_all, lax.all_gather(out_weight, 'tm', axis=1, tiled=True...  8.94 us
  transfers between devices with their start and end apart: 10, of which 4 were waited for; matrix products, arithmetic and copies ran while one was open for 7% of the time, Pallas kernels for 0%

commit v1 on v0

--- a/solution.py
+++ b/solution.py
@@ -6,6 +6,14 @@
 
 HD = 128
 WIN = 4
+
+
+def gather_from_all(shard, axis, dim):
+    size = lax.axis_size(axis)
+    repeats = [size if d == dim else 1 for d in range(shard.ndim)]
+    return lax.all_to_all(
+        jnp.tile(shard, repeats), axis, split_axis=dim, concat_axis=dim, tiled=True
+    )
 
 
 def from_behind(value, axis, steps):
@@ -21,7 +29,7 @@
     scale = 1.0 / math.sqrt(HD)
     position = lax.axis_index("tm")
     text_k, text_v = (
-        lax.all_gather(text_keys, "tm", axis=0, tiled=True),
+        gather_from_all(text_keys, "tm", 0),
         lax.all_gather(text_values, "tm", axis=0, tiled=True),
     )
     key_list = [keys]

time: 301 us -> 289 us (0.960)
  blocking collectives: 123 us -> 90.8 us
  local copies, waits for them, and re-layouts: 15.4 us -> 27.9 us
  starting transfers between devices: 27.5 us -> 36.8 us
  waiting for transfers between devices: 94.2 us -> 85.2 us
  matrix products: 17.1 us -> 23.5 us
    all_gather x1 -> x0, blocking collectives: 74.3 us -> none  [on_device(): lax.all_gather(text_keys, 'tm', axis=0, tiled=True)]
    all_gather x1, blocking collectives: 48.6 us -> 90.8 us  [on_device(): lax.all_gather(text_values, 'tm', axis=0, tiled=True)]
    unnamed x21, local copies, waits for them, and re-layouts: 12.2 us -> 21.1 us
    all_to_all x0 -> x1, starting transfers between devices: none -> 8.38 us  [gather_from_all(): lax.all_to_all(jnp.tile(shard, repeats), axis, split_axis=dim, concat_axi...]
    ppermute x8, waiting for transfers between devices: 24.2 us -> 16.2 us  [from_behind(): lax.ppermute(value, axis, [(source, source + steps) for source in range(i...]
    dot_general x5, matrix products: 3.71 us -> 9.22 us  [on_device(): jnp.dot(weights.astype(jnp.bfloat16), value_h, preferred_element_type=jnp...]
  transfers between devices with their start and end apart: 10 -> 11, of which waited for: 4 -> 3; matrix products, arithmetic and copies ran while one was open for 7% -> 14% of each run, Pallas kernels for 0% -> 0%
where the time goes in v1:
time: 289 us; the launch traced here: 287 us
  blocking collectives  90.8 us (31%)
  waiting for transfers between devices  85.2 us (29%)
  starting transfers between devices  36.8 us (13%)
  local copies, waits for them, and re-layouts  27.9 us (10%)
  matrix products  23.5 us (8%)
  between operations  16.8 us (6%)
  other arithmetic  6.31 us (2%)
    all_gather x1, blocking collectives, on_device(): lax.all_gather(text_values, 'tm', axis=0, tiled=True)  90.8 us
    unnamed x3, waiting for transfers between devices  69 us
    ppermute x8, starting transfers between devices, from_behind(): lax.ppermute(value, axis, [(source, source + steps) for source in range(i...  28.4 us
    unnamed x21, local copies, waits for them, and re-layouts  21.1 us
    ppermute x8, waiting for transfers between devices, from_behind(): lax.ppermute(value, axis, [(source, source + steps) for source in range(i...  16.2 us
    dot_general x5, matrix products, on_device(): jnp.dot(weights.astype(jnp.bfloat16), value_h, preferred_element_type=jnp...  9.22 us
    dot_general x1, matrix products, on_device(): jnp.dot(attended_all, lax.all_gather(out_weight, 'tm', axis=1, tiled=True...  8.93 us
    all_to_all x1, starting transfers between devices, gather_from_all(): lax.all_to_all(jnp.tile(shard, repeats), axis, split_axis=dim, concat_axi...  8.38 us
  transfers between devices with their start and end apart: 11, of which 3 were waited for; matrix products, arithmetic and copies ran while one was open for 14% of the time, Pallas kernels for 0%

profile of v1, /device:TPU:1, one launch (start us, length us, event | category | flops | bytes accessed | tf_op | source)
XLA Modules:
  0.0 287.2 jit_solution(8477077985667173023)
XLA Ops:
  6.5 0.7 all-gather.2.cloned.1.call-update
  7.3 4.5 %collective-permute-start = (bf16[384,640]{1,0:T(8,128)(2,1)}, bf16[384,640]{1,0:T(8,128)(2,1)}, u32[]{:S(2)}, u32[]{:S(2)}) collective-permute-start(bf16[384,640]{1,0:T(8,128)(2,1)} %param.9), channel_id=1, source_target_pairs={{0,8},{8,16},{16,24},{24,32},{32,40},{40,48},{48,56},{56,64},{64,7... | collective-permute-start | bytes 1474568 | tf_op jit(solution)/shard_map/ppermute | solution.py:22
  11.8 3.9 %collective-permute-start.1 = (bf16[384,640]{1,0:T(8,128)(2,1)}, bf16[384,640]{1,0:T(8,128)(2,1)}, u32[]{:S(2)}, u32[]{:S(2)}) collective-permute-start(bf16[384,640]{1,0:T(8,128)(2,1)} %param.9), channel_id=1, source_target_pairs={{0,16},{8,24},{16,32},{24,40},{32,48},{40,56},{48,64},{56,72},{64,... | collective-permute-start | bytes 1474568 | tf_op jit(solution)/shard_map/ppermute | solution.py:22
  15.7 3.5 %collective-permute-start.2 = (bf16[384,640]{1,0:T(8,128)(2,1)}, bf16[384,640]{1,0:T(8,128)(2,1)}, u32[]{:S(2)}, u32[]{:S(2)}) collective-permute-start(bf16[384,640]{1,0:T(8,128)(2,1)} %param.9), channel_id=1, source_target_pairs={{0,24},{8,32},{16,40},{24,48},{32,56},{40,64},{48,72},{56,80},{64,... | collective-permute-start | bytes 1474568 | tf_op jit(solution)/shard_map/ppermute | solution.py:22
  19.2 3.5 %collective-permute-start.3 = (bf16[384,640]{1,0:T(8,128)(2,1)}, bf16[384,640]{1,0:T(8,128)(2,1)}, u32[]{:S(2)}, u32[]{:S(2)}) collective-permute-start(bf16[384,640]{1,0:T(8,128)(2,1)} %param.9), channel_id=1, source_target_pairs={{0,32},{8,40},{16,48},{24,56},{32,64},{40,72},{48,80},{56,88},{64,... | collective-permute-start | bytes 1474568 | tf_op jit(solution)/shard_map/ppermute | solution.py:22
  22.6 1.6 tile.2
  24.3 8.4 %all-to-all-start = ((bf16[64,8,640]{2,1,0:T(8,128)(2,1)}), bf16[64,8,640]{2,1,0:T(8,128)(2,1)}, u32[]{:S(2)}, u32[]{:S(2)}) async-start(bf16[64,8,640]{2,1,0:T(8,128)(2,1)} %tile.2), calls=%async_computation | async-start | bytes 1310720 | tf_op jit(solution)/shard_map/all_to_all | solution.py:14
  32.7 3.5 %collective-permute-start.4 = (bf16[384,640]{1,0:T(8,128)(2,1)}, bf16[384,640]{1,0:T(8,128)(2,1)}, u32[]{:S(2)}, u32[]{:S(2)}) collective-permute-start(bf16[384,640]{1,0:T(8,128)(2,1)} %param.10), channel_id=1, source_target_pairs={{0,8},{8,16},{16,24},{24,32},{32,40},{40,48},{48,56},{56,64},{64,7... | collective-permute-start | bytes 1474568 | tf_op jit(solution)/shard_map/ppermute | solution.py:22
  36.3 1.3 dynamic_slice.18
  38.8 1.5 fusion.95
  40.3 0.6 fusion.90
  41.0 1.1 constant_dynamic-update-slice_fusion.4
  42.1 90.8 %all_gather.6 = bf16[512,640]{1,0:T(8,128)(2,1)} all-gather(bf16[8,640]{1,0:T(8,128)(2,1)} %param.12), channel_id=1, replica_groups=mesh['tm'=64,'head'=8] {'tm'}, dimensions={0}, use_global_device_ids=true | all-gather | bytes 665600 | tf_op jit(solution)/shard_map/all_gather | solution.py:33
  132.8 0.6 fusion.91
  136.6 0.7 fusion.94
  138.6 1.9 constant_dynamic-update-slice_fusion.10
  140.5 1.4 collective-permute-start.5
  141.9 1.1 constant_dynamic-update-slice_fusion.3
  143.0 4.8 %collective-permute-start.6 = (bf16[384,640]{1,0:T(8,128)(2,1)}, bf16[384,640]{1,0:T(8,128)(2,1)S(1)}, u32[]{:S(2)}, u32[]{:S(2)}) collective-permute-start(bf16[384,640]{1,0:T(8,128)(2,1)} %param.10), channel_id=1, source_target_pairs={{0,24},{8,32},{16,40},{24,48},{32,56},{40,64},{48,72},{56,80},{64,... | collective-permute-start | bytes 1474568 | tf_op jit(solution)/shard_map/ppermute | solution.py:22
  147.8 1.1 constant_dynamic-update-slice_fusion.2
  148.9 3.2 %collective-permute-start.7 = (bf16[384,640]{1,0:T(8,128)(2,1)}, bf16[384,640]{1,0:T(8,128)(2,1)S(1)}, u32[]{:S(2)}, u32[]{:S(2)}) collective-permute-start(bf16[384,640]{1,0:T(8,128)(2,1)} %param.10), channel_id=1, source_target_pairs={{0,32},{8,40},{16,48},{24,56},{32,64},{40,72},{48,80},{56,88},{64,... | collective-permute-start | bytes 1474568 | tf_op jit(solution)/shard_map/ppermute | solution.py:22
  152.1 1.1 constant_dynamic-update-slice_fusion.1
  153.2 1.1 constant_dynamic-update-slice_fusion
  154.3 1.9 constant_dynamic-update-slice_fusion.9
  156.2 0.8 constant_dynamic-update-slice_fusion.8
  157.0 6.5 %collective-permute-done.6 = bf16[384,640]{1,0:T(8,128)(2,1)S(1)} collective-permute-done((bf16[384,640]{1,0:T(8,128)(2,1)}, bf16[384,640]{1,0:T(8,128)(2,1)S(1)}, u32[]{:S(2)}, u32[]{:S(2)}) %collective-permute-start.6) | collective-permute-done | bytes 491552 | tf_op jit(solution)/shard_map/ppermute | solution.py:22
  163.5 0.9 constant_dynamic-update-slice_fusion.7
  164.4 9.7 %collective-permute-done.7 = bf16[384,640]{1,0:T(8,128)(2,1)S(1)} collective-permute-done((bf16[384,640]{1,0:T(8,128)(2,1)}, bf16[384,640]{1,0:T(8,128)(2,1)S(1)}, u32[]{:S(2)}, u32[]{:S(2)}) %collective-permute-start.7) | collective-permute-done | bytes 491552 | tf_op jit(solution)/shard_map/ppermute | solution.py:22
  174.0 0.9 constant_dynamic-update-slice_fusion.6
  174.9 1.0 constant_dynamic-update-slice_fusion.5
  175.9 1.2 bitcast_dynamic-update-slice_fusion
  177.1 1.8 fusion.96
  179.5 0.9 fusion.97
  180.4 0.6 fusion.7
  181.0 0.9 fusion.98
  181.9 0.6 fusion.9
  182.5 0.9 fusion.99
  184.0 0.9 fusion.100
  184.9 0.6 fusion.13
  185.5 1.9 fusion.72
  187.4 1.8 fusion.66
  189.2 1.8 fusion.60
  191.1 1.8 fusion.54
  192.9 1.8 fusion.48
  194.8 8.9 %convolution_convert_fusion = bf16[384,5120]{1,0:T(8,128)(2,1)} fusion(bf16[384,640]{1,0:T(8,128)(2,1)S(1)} %fusion.48, bf16[640,5120]{0,1:T(8,128)(2,1)} %all-gather.2.cloned.1.call-done), kind=kOutput, calls=%fused_computation | convolution fusion | flops 2518548480 | bytes 10977280 | tf_op jit(solution)/shard_map/dot_general | solution.py:75
  203.8 6.3 %copy.9 = bf16[384,5120]{0,1:T(8,128)(2,1)} copy(bf16[384,5120]{1,0:T(8,128)(2,1)} %convolution_convert_fusion) | data formatting | bytes 7864320
  210.0 68.3 %reduce-scatter.4.cloned.1.call-done = bf16[640,384]{1,0:T(8,128)(2,1)} async-done(((bf16[5120,384]{1,0:T(8,128)(2,1)}), bf16[640,384]{1,0:T(8,128)(2,1)}) %reduce-scatter.4.cloned.1.call-update) | async-done | bytes 491536
  278.4 2.0 copy.10
  (27 shorter events, 3.9 us)
Async XLA Ops:
  6.5 188.3 %all-gather.2.cloned.1.call-start = ((), (), s32[]{:S(2)}) async-start(), calls=%async_computation.2 | async-start | bytes 6656000 | tf_op jit(solution)/shard_map/all_gather | solution.py:77
  7.3 133.2 %collective-permute-start = (bf16[384,640]{1,0:T(8,128)(2,1)}, bf16[384,640]{1,0:T(8,128)(2,1)}, u32[]{:S(2)}, u32[]{:S(2)}) collective-permute-start(bf16[384,640]{1,0:T(8,128)(2,1)} %param.9), channel_id=1, source_target_pairs={{0,8},{8,16},{16,24},{24,32},{32,40},{40,48},{48,56},{56,64},{64,7... | collective-permute-start | bytes 1474568 | tf_op jit(solution)/shard_map/ppermute | solution.py:22
  11.8 131.2 %collective-permute-start.1 = (bf16[384,640]{1,0:T(8,128)(2,1)}, bf16[384,640]{1,0:T(8,128)(2,1)}, u32[]{:S(2)}, u32[]{:S(2)}) collective-permute-start(bf16[384,640]{1,0:T(8,128)(2,1)} %param.9), channel_id=1, source_target_pairs={{0,16},{8,24},{16,32},{24,40},{32,48},{40,56},{48,64},{56,72},{64,... | collective-permute-start | bytes 1474568 | tf_op jit(solution)/shard_map/ppermute | solution.py:22
  15.7 133.2 %collective-permute-start.2 = (bf16[384,640]{1,0:T(8,128)(2,1)}, bf16[384,640]{1,0:T(8,128)(2,1)}, u32[]{:S(2)}, u32[]{:S(2)}) collective-permute-start(bf16[384,640]{1,0:T(8,128)(2,1)} %param.9), channel_id=1, source_target_pairs={{0,24},{8,32},{16,40},{24,48},{32,56},{40,64},{48,72},{56,80},{64,... | collective-permute-start | bytes 1474568 | tf_op jit(solution)/shard_map/ppermute | solution.py:22
  19.2 134.1 %collective-permute-start.3 = (bf16[384,640]{1,0:T(8,128)(2,1)}, bf16[384,640]{1,0:T(8,128)(2,1)}, u32[]{:S(2)}, u32[]{:S(2)}) collective-permute-start(bf16[384,640]{1,0:T(8,128)(2,1)} %param.9), channel_id=1, source_target_pairs={{0,32},{8,40},{16,48},{24,56},{32,64},{40,72},{48,80},{56,88},{64,... | collective-permute-start | bytes 1474568 | tf_op jit(solution)/shard_map/ppermute | solution.py:22
  24.3 151.6 %all-to-all-start = ((bf16[64,8,640]{2,1,0:T(8,128)(2,1)}), bf16[64,8,640]{2,1,0:T(8,128)(2,1)}, u32[]{:S(2)}, u32[]{:S(2)}) async-start(bf16[64,8,640]{2,1,0:T(8,128)(2,1)} %tile.2), calls=%async_computation | async-start | bytes 1310720 | tf_op jit(solution)/shard_map/all_to_all | solution.py:14
  32.6 245.7 %reduce-scatter.4.cloned.1.call-start = ((), (), s32[]{:S(2)}) async-start(), calls=%async_computation.3 | async-start | bytes 4423680
  32.7 121.6 %collective-permute-start.4 = (bf16[384,640]{1,0:T(8,128)(2,1)}, bf16[384,640]{1,0:T(8,128)(2,1)}, u32[]{:S(2)}, u32[]{:S(2)}) collective-permute-start(bf16[384,640]{1,0:T(8,128)(2,1)} %param.10), channel_id=1, source_target_pairs={{0,8},{8,16},{16,24},{24,32},{32,40},{40,48},{48,56},{56,64},{64,7... | collective-permute-start | bytes 1474568 | tf_op jit(solution)/shard_map/ppermute | solution.py:22
  140.5 34.4 %copy-start = (bf16[512,640]{1,0:T(8,128)(2,1)S(1)}, bf16[512,640]{1,0:T(8,128)(2,1)}, u32[]{:S(2)}) copy-start(bf16[512,640]{1,0:T(8,128)(2,1)} %all_gather.6) | copy-start | bytes 1966084
  140.5 15.7 %collective-permute-start.5 = (bf16[384,640]{1,0:T(8,128)(2,1)}, bf16[384,640]{1,0:T(8,128)(2,1)S(1)}, u32[]{:S(2)}, u32[]{:S(2)}) collective-permute-start(bf16[384,640]{1,0:T(8,128)(2,1)} %param.10), channel_id=1, source_target_pairs={{0,16},{8,24},{16,32},{24,40},{32,48},{40,56},{48,64},{56,72},{64,... | collective-permute-start | bytes 1474568 | tf_op jit(solution)/shard_map/ppermute | solution.py:22
  143.0 20.5 %collective-permute-start.6 = (bf16[384,640]{1,0:T(8,128)(2,1)}, bf16[384,640]{1,0:T(8,128)(2,1)S(1)}, u32[]{:S(2)}, u32[]{:S(2)}) collective-permute-start(bf16[384,640]{1,0:T(8,128)(2,1)} %param.10), channel_id=1, source_target_pairs={{0,24},{8,32},{16,40},{24,48},{32,56},{40,64},{48,72},{56,80},{64,... | collective-permute-start | bytes 1474568 | tf_op jit(solution)/shard_map/ppermute | solution.py:22
  148.9 25.1 %collective-permute-start.7 = (bf16[384,640]{1,0:T(8,128)(2,1)}, bf16[384,640]{1,0:T(8,128)(2,1)S(1)}, u32[]{:S(2)}, u32[]{:S(2)}) collective-permute-start(bf16[384,640]{1,0:T(8,128)(2,1)} %param.10), channel_id=1, source_target_pairs={{0,32},{8,40},{16,48},{24,56},{32,64},{40,72},{48,80},{56,88},{64,... | collective-permute-start | bytes 1474568 | tf_op jit(solution)/shard_map/ppermute | solution.py:22
  177.0 2.5 copy-start.1
Sparse Core Ops, SparseCore 0:
  10.6 115.6 all-gather.1
  210.2 68.1 reduce-scatter.3
